TPU v7x, 256 devices: a whole 4x4x8 slice. The times are simulated.
256 devices in a mesh: kv: 8 (over z), blk: 32 (over y, x, core).
Axes of the slice: x: 4, y: 4, z: 8, core: 2. Of those that a mesh axis runs over, the one named last changes fastest.
Arguments:
- embeds: bfloat16 [1, 256, 3072], P(None, None, 'blk'), may hold values from -40 to 40
- attn_norm: float32 [3072], P('blk'), may hold values from 0.25 to 1.75
- query_key_value_weight: bfloat16 [3072, 5120], P('blk', 'kv'), may hold values from -0.109375 to 0.109375
- w_out: bfloat16 [3072, 3072], P('kv', 'blk'), may hold values from -0.109375 to 0.109375
- mlp_norm: float32 [3072], P('blk'), may hold values from 0.25 to 1.75
- w_gate: bfloat16 [3072, 8192], P('blk', 'kv'), may hold values from -0.109375 to 0.109375
- w_up: bfloat16 [3072, 8192], P('blk', 'kv'), may hold values from -0.109375 to 0.109375
- w_down: bfloat16 [8192, 3072], P('kv', 'blk'), may hold values from -0.0625 to 0.0625
- prompt_key_slots: bfloat16 [256, 8, 128, 128], P('blk', 'kv'), may hold values from -210 to 210
- prompt_value_slots: bfloat16 [256, 8, 128, 128], P('blk', 'kv'), may hold values from -6 to 6
- generated_keys: bfloat16 [256, 8, 127, 128], P('blk', 'kv'), may hold values from -10 to 10
- generated_values: bfloat16 [256, 8, 127, 128], P('blk', 'kv'), may hold values from -6 to 6
- parents: int32 [1, 256], P(None, 'blk'), may hold values from 0 to 7
- prompt_length: int32 [32], replicated, may hold values from 1024 to 8192
- tenant_bounds: int32 [5], replicated, may hold values from 0 to 32, as said below
- slot_table: int32 [256], P('blk'), may hold values from 0 to 256, as said below
Outputs:
- hidden_out: float32 [1, 256, 3072], P(None, None, 'blk')
- keys_out: bfloat16 [256, 8, 128, 128], P('blk', 'kv')
- values_out: bfloat16 [256, 8, 128, 128], P('blk', 'kv')
Inputs may be any that keep to these rules, and one draw needn't show every extreme that they name: parents[s, b] is the beam, among the 8 beams of b's request, whose cache beam b continues at step s. tenant_bounds[0] = 0 and tenant_bounds[4] = 32, strictly rising. `slot_table`: with L_t the largest prompt_length of tenant t's requests, every block j below ceil(L_t / 128) of every tenant t stands in exactly one slot as t * 64 + j, no other block stands anywhere, and 256 marks an empty slot.
All inputs are finite; a program needn't handle non-finite values.
Results may differ from a plain program's by a relative error of at most 0.012.
The roundings to bfloat16 on the way count: a program that leaves them out, or rounds other values in their place, can miss the bound.
Values may be sent and summed in bfloat16 or wider, within the bound.
No kernel may reach another device: no remote copies, remote signals or barrier semaphores. Data moves between devices by JAX's collectives and lax.ppermute only.
A program may use at most 64 MiB of HBM per device.

v0:
```python
import math
import jax
import jax.numpy as jnp
from jax import lax
from jax.sharding import PartitionSpec as P

MODEL_WIDTH = 3072
QUERY_HEADS = 24
KEY_VALUE_HEADS = 8
HEAD_WIDTH = 128
REQUEST_BEAMS = 8
TENANT_COUNT = 4
BLOCK_POSITIONS = 128
PROMPT_BLOCKS = 64
EARLIER_TOKENS = 127
DECODE_STEPS = 1
masked_score = -1e30


def exchange(value, axis, bit):
    count = lax.axis_size(axis)
    return lax.ppermute(value, axis, [(i, i ^ 1 << bit) for i in range(count)])


def butterfly_sum(value, axis):
    count = lax.axis_size(axis)
    if count & count - 1:
        return lax.psum(value, axis)
    for bit in range(count.bit_length() - 1):
        value = value + exchange(value, axis, bit)
    return value


def scatter_sum(value, axis):
    count = lax.axis_size(axis)
    pieces = value.reshape((count, value.shape[0] // count) + value.shape[1:])
    return jnp.sum(lax.all_to_all(pieces, axis, 0, 0, tiled=False), axis=0)


def rotate(values, angles):
    half = values.shape[-1] // 2
    first = values[..., :half]
    second = values[..., half:]
    cosine = jnp.cos(angles)
    sine = jnp.sin(angles)
    return jnp.concatenate(
        [first * cosine - second * sine, second * cosine + first * sine], axis=-1
    )


def angles_for(positions, head_size):
    half = head_size // 2
    freq = jnp.exp(jnp.arange(half, dtype=jnp.float32) * (-math.log(500000.0) / half))
    return positions.astype(jnp.float32)[:, None] * freq[None, :]


def across_heads(partial_value):
    return butterfly_sum(partial_value, "kv")


def body(
    embeds,
    attn_norm,
    query_key_value_weight,
    w_out,
    mlp_norm,
    w_gate,
    w_up,
    w_down,
    prompt_key_slots,
    prompt_value_slots,
    generated_keys,
    generated_values,
    parents,
    prompt_length,
    tenant_bounds,
    slot_table,
):
    blocks = lax.axis_size("blk")
    my_index = lax.axis_index("blk")
    all_rows = embeds.shape[1]
    own_rows = all_rows // blocks
    heads_kv = prompt_key_slots.shape[1]
    slots_here = prompt_key_slots.shape[0]
    keys_here = slots_here * BLOCK_POSITIONS
    group_queries = QUERY_HEADS // KEY_VALUE_HEADS
    col_width = group_queries + 2
    score_scale = 1.0 / math.sqrt(HEAD_WIDTH)
    unit_count = w_gate.shape[1]
    beam_req = jnp.arange(all_rows, dtype=jnp.int32) // REQUEST_BEAMS
    tenant_beam = jnp.sum(
        (beam_req[:, None] >= tenant_bounds[None, 1:TENANT_COUNT]).astype(jnp.int32), axis=1
    )
    length_beam = jnp.repeat(prompt_length, REQUEST_BEAMS)
    slot_tenant = jnp.repeat(slot_table // PROMPT_BLOCKS, BLOCK_POSITIONS)
    slot_pos = jnp.repeat(slot_table % PROMPT_BLOCKS * BLOCK_POSITIONS, BLOCK_POSITIONS) + jnp.tile(
        jnp.arange(BLOCK_POSITIONS, dtype=jnp.int32), slots_here
    )
    visible = (tenant_beam[:, None] == slot_tenant[None, :]) & (
        slot_pos[None, :] < length_beam[:, None]
    )
    prompt_mask = visible[None, :, None, :]
    keys_flat = prompt_key_slots.transpose(1, 0, 2, 3).reshape(heads_kv, keys_here, HEAD_WIDTH)
    values_flat = prompt_value_slots.transpose(1, 0, 2, 3).reshape(heads_kv, keys_here, HEAD_WIDTH)
    local_beam = jnp.arange(own_rows, dtype=jnp.int32)
    base_rows = local_beam // REQUEST_BEAMS * REQUEST_BEAMS
    trailing_zeros = jnp.zeros((own_rows, heads_kv, DECODE_STEPS, HEAD_WIDTH), jnp.bfloat16)
    cached_key_rows = jnp.concatenate([generated_keys, trailing_zeros], axis=2)
    cached_value_rows = jnp.concatenate([generated_values, trailing_zeros], axis=2)
    gen_pos = jnp.arange(EARLIER_TOKENS + DECODE_STEPS, dtype=jnp.int32)
    w_both = jnp.concatenate([w_gate, w_up], axis=1)
    residual = embeds[0].astype(jnp.float32)
    squares = jnp.sum(residual * residual, axis=1)
    normed = (residual * attn_norm).astype(jnp.bfloat16)
    partial_value = jnp.dot(normed, query_key_value_weight, preferred_element_type=jnp.float32)
    own_value = scatter_sum(jnp.concatenate([partial_value, squares[:, None]], axis=1), "blk")
    inverse = lax.rsqrt(own_value[:, -1] / MODEL_WIDTH + 1e-05)
    own_proj = (own_value[:, :-1] * inverse[:, None]).reshape(
        own_rows, heads_kv, col_width, HEAD_WIDTH
    )
    own_length = lax.dynamic_slice_in_dim(length_beam, my_index * own_rows, own_rows, 0)
    own_angle = angles_for(own_length + EARLIER_TOKENS + 0, HEAD_WIDTH)
    own_queries = rotate(own_proj[:, :, :group_queries], own_angle[:, None, None, :]).astype(
        jnp.bfloat16
    )
    query_rows = lax.all_gather(own_queries, "blk", axis=0, tiled=True)
    new_key = rotate(own_proj[:, :, group_queries], own_angle[:, None, :]).astype(jnp.bfloat16)
    new_value = own_proj[:, :, group_queries + 1].astype(jnp.bfloat16)
    parent_rows = base_rows + parents[0]
    cached_key_rows = (
        jnp.take(cached_key_rows, parent_rows, axis=0).at[:, :, EARLIER_TOKENS].set(new_key)
    )
    cached_value_rows = (
        jnp.take(cached_value_rows, parent_rows, axis=0).at[:, :, EARLIER_TOKENS].set(new_value)
    )
    grouped = query_rows.transpose(1, 0, 2, 3).reshape(
        heads_kv, all_rows * group_queries, HEAD_WIDTH
    )
    scores = jnp.einsum("kqd,knd->kqn", grouped, keys_flat, preferred_element_type=jnp.float32)
    scores = scores.reshape(heads_kv, all_rows, group_queries, keys_here) * score_scale
    top_score = jnp.max(jnp.where(prompt_mask, scores, masked_score), axis=3)
    weights = jnp.where(prompt_mask, jnp.exp(scores - top_score[..., None]), 0.0)
    total_mass = jnp.sum(weights, axis=3)
    flat_weights = weights.reshape(heads_kv, all_rows * group_queries, keys_here).astype(
        jnp.bfloat16
    )
    summed = jnp.einsum(
        "kqn,knd->kqd", flat_weights, values_flat, preferred_element_type=jnp.float32
    )
    summed = summed.reshape(heads_kv, all_rows, group_queries, HEAD_WIDTH)
    packed = jnp.concatenate([summed, top_score[..., None], total_mass[..., None]], axis=3)
    packed = packed.transpose(1, 0, 2, 3).reshape(
        blocks, own_rows, heads_kv, group_queries, HEAD_WIDTH + 2
    )
    parts = lax.all_to_all(packed, "blk", 0, 0, tiled=False)
    part_top = parts[..., HEAD_WIDTH]
    prompt_top = jnp.max(part_top, axis=0)
    part_factor = jnp.exp(part_top - prompt_top[None])
    prompt_mass = jnp.sum(parts[..., HEAD_WIDTH + 1] * part_factor, axis=0)
    prompt_sum = jnp.sum(parts[..., :HEAD_WIDTH] * part_factor[..., None], axis=0)
    prompt_top = prompt_top.transpose(1, 0, 2)
    prompt_mass = prompt_mass.transpose(1, 0, 2)
    prompt_sum = prompt_sum.transpose(1, 0, 2, 3)
    gen_scores = (
        jnp.einsum(
            "bkgd,bknd->kbgn", own_queries, cached_key_rows, preferred_element_type=jnp.float32
        )
        * score_scale
    )
    live = (gen_pos <= EARLIER_TOKENS)[None, None, None, :]
    gen_top = jnp.max(jnp.where(live, gen_scores, masked_score), axis=3)
    best = jnp.maximum(prompt_top, gen_top)
    gen_weights = jnp.where(live, jnp.exp(gen_scores - best[..., None]), 0.0)
    shift = jnp.exp(prompt_top - best)
    full_mass = prompt_mass * shift + jnp.sum(gen_weights, axis=3)
    gen_sum = jnp.einsum(
        "kbgn,bknd->kbgd",
        gen_weights.astype(jnp.bfloat16),
        cached_value_rows,
        preferred_element_type=jnp.float32,
    )
    attended_output = (prompt_sum * shift[..., None] + gen_sum) / full_mass[..., None]
    heads_out = (
        attended_output.transpose(1, 0, 2, 3)
        .reshape(own_rows, heads_kv * group_queries * HEAD_WIDTH)
        .astype(jnp.bfloat16)
    )
    head_part = jnp.dot(
        lax.all_gather(heads_out, "blk", axis=0, tiled=True),
        w_out,
        preferred_element_type=jnp.float32,
    )
    after_attn = residual + across_heads(head_part)
    squares2 = jnp.sum(after_attn * after_attn, axis=1)
    normed2 = (after_attn * mlp_norm).astype(jnp.bfloat16)
    mixed = scatter_sum(
        jnp.concatenate(
            [jnp.dot(normed2, w_both, preferred_element_type=jnp.float32), squares2[:, None]],
            axis=1,
        ),
        "blk",
    )
    own_inverse = lax.rsqrt(mixed[:, -1] / MODEL_WIDTH + 1e-05)
    gate = mixed[:, :unit_count] * own_inverse[:, None]
    upper = mixed[:, unit_count : 2 * unit_count] * own_inverse[:, None]
    hidden = (jax.nn.silu(gate) * upper).astype(jnp.bfloat16)
    ff_part = jnp.dot(
        lax.all_gather(hidden, "blk", axis=0, tiled=True),
        w_down,
        preferred_element_type=jnp.float32,
    )
    outputs = [after_attn + across_heads(ff_part)]
    return (jnp.stack(outputs), cached_key_rows, cached_value_rows)


def solution(mesh):
    in_specs = (
        P(None, None, "blk"),
        P("blk"),
        P("blk", "kv"),
        P("kv", "blk"),
        P("blk"),
        P("blk", "kv"),
        P("blk", "kv"),
        P("kv", "blk"),
        P("blk", "kv", None, None),
        P("blk", "kv", None, None),
        P("blk", "kv", None, None),
        P("blk", "kv", None, None),
        P(None, "blk"),
        P(),
        P(),
        P("blk"),
    )
    out_specs = (P(None, None, "blk"), P("blk", "kv", None, None), P("blk", "kv", None, None))
    return jax.shard_map(body, mesh=mesh, in_specs=in_specs, out_specs=out_specs, check_vma=False)
```

profile of v0, /device:TPU:2, one launch (start us, length us, event | category | flops | bytes accessed | tf_op | source)
XLA Modules:
  0.0 210.3 jit_solution(3467085731439705462)
XLA Ops:
  0.7 1.0 copy.159
  1.7 0.8 fusion.23
  2.5 0.2 concatenate.90
  2.7 1.1 fusion.21
  3.9 0.9 pad_maximum_fusion.1
  4.8 7.6 %all-to-all-start = ((f32[32,8,641]{2,1,0:T(8,128)}), f32[32,8,641]{2,1,0:T(8,128)S(1)}, u32[]{:S(2)}, u32[]{:S(2)}) async-start(f32[32,8,641]{2,1,0:T(8,128)} %pad_maximum_fusion.1), calls=%async_computation | async-start | bytes 1572864 | tf_op jit(solution)/shard_map/all_to_all | solution.py:37
  12.6 0.1 lt.33
  13.0 0.1 multiply_cosine_fusion.1
  13.3 0.6 gather_fusion
  13.9 0.6 gather_fusion.1
  14.5 0.1 convert_reduce_fusion
  14.6 1.0 compare_and_fusion
  15.5 0.9 bitcast_select_fusion.1
  16.4 9.3 %all-to-all-done = f32[32,8,641]{2,1,0:T(8,128)S(1)} async-done(((f32[32,8,641]{2,1,0:T(8,128)}), f32[32,8,641]{2,1,0:T(8,128)S(1)}, u32[]{:S(2)}, u32[]{:S(2)}) %all-to-all-start) | async-done | bytes 656416 | tf_op jit(solution)/shard_map/all_to_all | solution.py:37
  25.8 0.1 fusion.53
  26.2 22.9 %all_gather.9 = bf16[256,1,3,128]{3,0,2,1:T(8,128)(2,1)S(1)} all-gather(bf16[8,1,3,128]{3,0,2,1:T(8,128)(2,1)S(1)} %pad_maximum_fusion.2), channel_id=1, replica_groups=mesh['kv'=8,'blk'=32] {'blk'}, dimensions={0}, use_global_device_ids=true | all-gather | bytes 202752 | tf_op jit(solution)/shard_map/all_gather | solution.py:126
  49.0 1.8 select_reduce_fusion
  50.8 0.1 concatenate.75
  50.9 3.1 %fusion.2 = (bf16[32,8,3,1024]{3,1,0,2:T(8,128)(2,1)}, f32[256,3]{0,1:T(4,128)S(1)}) fusion(f32[256,3,1024]{2,0,1:T(8,128)S(1)} %get-tuple-element.71, f32[256,3]{0,1:T(4,128)S(1)} %get-tuple-element.70, pred[256,1024]{1,0:T(8,128)(4,1)} %compare_and_fusion), kind=kLoop, calls=%fused_computation.8 | loop fusion | flops 3931392 | bytes 4986880 | tf_op jit(solution)/shard_map/reshape.462
  54.0 0.1 concatenate.76
  54.1 0.6 copy.163
  54.7 0.6 copy.162
  55.4 2.0 fusion.5
  57.4 1.1 maximum_bitcast_fusion
  58.5 5.7 %all-to-all-start.1 = ((f32[32,8,1,3,130]{4,1,3,2,0:T(8,128)}), f32[32,8,1,3,130]{4,1,3,2,0:T(8,128)S(1)}, u32[]{:S(2)}, u32[]{:S(2)}) async-start(f32[32,8,1,3,130]{4,1,3,2,0:T(8,128)} %maximum_bitcast_fusion), calls=%async_computation.1 | async-start | bytes 1572864 | tf_op jit(solution)/shard_map/all_to_all | solution.py:155
  64.2 0.1 fusion.55
  64.6 0.3 select_reduce_fusion.1
  64.9 0.1 copy.172
  65.1 12.5 %all-to-all-done.1 = f32[32,8,1,3,130]{4,1,3,2,0:T(8,128)S(1)} async-done(((f32[32,8,1,3,130]{4,1,3,2,0:T(8,128)}), f32[32,8,1,3,130]{4,1,3,2,0:T(8,128)S(1)}, u32[]{:S(2)}, u32[]{:S(2)}) %all-to-all-start.1) | async-done | bytes 399392 | tf_op jit(solution)/shard_map/all_to_all | solution.py:155
  77.5 0.2 fusion.61
  77.7 0.2 copy.185
  78.0 0.2 copy.186
  78.3 0.2 fusion.32
  78.4 0.1 copy.175
  78.5 0.2 fusion.33
  78.7 0.1 copy.179
  78.8 0.1 copy.173
  78.9 0.1 copy.166
  79.0 0.2 fusion.12
  79.2 0.2 fusion.10
  79.5 23.1 %all_gather.10 = bf16[256,384]{1,0:T(8,128)(2,1)S(1)} all-gather(bf16[8,384]{1,0:T(8,128)(2,1)S(1)} %bitcast.108), channel_id=1, replica_groups=mesh['kv'=8,'blk'=32] {'blk'}, dimensions={0}, use_global_device_ids=true | all-gather | bytes 202752 | tf_op jit(solution)/shard_map/all_gather | solution.py:189
  102.6 0.2 fusion.62
  102.8 2.0 collective-permute-start
  104.8 3.3 %collective-permute-done = f32[256,96]{0,1:T(8,128)S(1)} collective-permute-done((f32[256,96]{0,1:T(8,128)S(1)}, f32[256,96]{0,1:T(8,128)S(1)}, u32[]{:S(2)}, u32[]{:S(2)}) %collective-permute-start) | collective-permute-done | bytes 98336 | tf_op jit(solution)/shard_map/ppermute | solution.py:22
  108.1 3.4 %collective-permute-start.1 = (f32[256,96]{0,1:T(8,128)S(1)}, f32[256,96]{0,1:T(8,128)S(1)}, u32[]{:S(2)}, u32[]{:S(2)}) collective-permute-start(f32[256,96]{0,1:T(8,128)S(1)} %add.109), channel_id=1, source_target_pairs={{0,64},{32,96},{64,0},{96,32},{128,192},{160,224},{192,128},{224,1... | collective-permute-start | bytes 294920 | tf_op jit(solution)/shard_map/ppermute | solution.py:22
  111.4 4.8 %collective-permute-done.1 = f32[256,96]{0,1:T(8,128)S(1)} collective-permute-done((f32[256,96]{0,1:T(8,128)S(1)}, f32[256,96]{0,1:T(8,128)S(1)}, u32[]{:S(2)}, u32[]{:S(2)}) %collective-permute-start.1) | collective-permute-done | bytes 98336 | tf_op jit(solution)/shard_map/ppermute | solution.py:22
  116.3 6.3 %collective-permute-start.2 = (f32[256,96]{0,1:T(8,128)S(1)}, f32[256,96]{0,1:T(8,128)S(1)}, u32[]{:S(2)}, u32[]{:S(2)}) collective-permute-start(f32[256,96]{0,1:T(8,128)S(1)} %add.110), channel_id=1, source_target_pairs={{0,128},{32,160},{64,192},{96,224},{128,0},{160,32},{192,64},{224,... | collective-permute-start | bytes 294920 | tf_op jit(solution)/shard_map/ppermute | solution.py:22
  122.5 3.6 %collective-permute-done.2 = f32[256,96]{0,1:T(8,128)S(1)} collective-permute-done((f32[256,96]{0,1:T(8,128)S(1)}, f32[256,96]{0,1:T(8,128)S(1)}, u32[]{:S(2)}, u32[]{:S(2)}) %collective-permute-start.2) | collective-permute-done | bytes 98336 | tf_op jit(solution)/shard_map/ppermute | solution.py:22
  126.2 0.2 concatenate.91
  126.5 0.5 convolution_bitcast_fusion
  127.0 0.2 pad_maximum_fusion
  127.2 34.6 %all_to_all.15 = f32[32,8,2049]{2,1,0:T(8,128)S(1)} all-to-all(f32[32,8,2049]{2,1,0:T(8,128)S(1)} %pad_maximum_fusion), channel_id=1, replica_groups=mesh['kv'=8,'blk'=32] {'blk'}, dimensions={0} | all-to-all | bytes 4196352 | tf_op jit(solution)/shard_map/all_to_all | solution.py:37
  161.8 0.1 reduce_sum.89
  161.9 0.1 fusion.50
  162.0 0.1 fusion.28
  162.1 23.3 %all_gather.11 = bf16[256,1024]{1,0:T(8,128)(2,1)S(1)} all-gather(bf16[8,1024]{1,0:T(8,128)(2,1)S(1)} %fusion.28), channel_id=1, replica_groups=mesh['kv'=8,'blk'=32] {'blk'}, dimensions={0}, use_global_device_ids=true | all-gather | bytes 540672 | tf_op jit(solution)/shard_map/all_gather | solution.py:208
  185.5 0.3 fusion.63
  185.8 0.1 collective-permute-start.3
  185.9 5.0 %collective-permute-done.3 = f32[256,96]{0,1:T(8,128)S(1)} collective-permute-done((f32[256,96]{0,1:T(8,128)S(1)}, f32[256,96]{0,1:T(8,128)S(1)}, u32[]{:S(2)}, u32[]{:S(2)}) %collective-permute-start.3) | collective-permute-done | bytes 98336 | tf_op jit(solution)/shard_map/ppermute | solution.py:22
  190.9 3.3 %collective-permute-start.4 = (f32[256,96]{0,1:T(8,128)S(1)}, f32[256,96]{0,1:T(8,128)S(1)}, u32[]{:S(2)}, u32[]{:S(2)}) collective-permute-start(f32[256,96]{0,1:T(8,128)S(1)} %add.115), channel_id=1, source_target_pairs={{0,64},{32,96},{64,0},{96,32},{128,192},{160,224},{192,128},{224,1... | collective-permute-start | bytes 294920 | tf_op jit(solution)/shard_map/ppermute | solution.py:22
  194.2 4.8 %collective-permute-done.4 = f32[256,96]{0,1:T(8,128)S(1)} collective-permute-done((f32[256,96]{0,1:T(8,128)S(1)}, f32[256,96]{0,1:T(8,128)S(1)}, u32[]{:S(2)}, u32[]{:S(2)}) %collective-permute-start.4) | collective-permute-done | bytes 98336 | tf_op jit(solution)/shard_map/ppermute | solution.py:22
  199.0 4.3 %collective-permute-start.5 = (f32[256,96]{0,1:T(8,128)S(1)}, f32[256,96]{0,1:T(8,128)S(1)}, u32[]{:S(2)}, u32[]{:S(2)}) collective-permute-start(f32[256,96]{0,1:T(8,128)S(1)} %add.116), channel_id=1, source_target_pairs={{0,128},{32,160},{64,192},{96,224},{128,0},{160,32},{192,64},{224,... | collective-permute-start | bytes 294920 | tf_op jit(solution)/shard_map/ppermute | solution.py:22
  203.4 6.2 %collective-permute-done.5 = f32[256,96]{0,1:T(8,128)S(1)} collective-permute-done((f32[256,96]{0,1:T(8,128)S(1)}, f32[256,96]{0,1:T(8,128)S(1)}, u32[]{:S(2)}, u32[]{:S(2)}) %collective-permute-start.5) | collective-permute-done | bytes 98336 | tf_op jit(solution)/shard_map/ppermute | solution.py:22
  209.6 0.7 add_bitcast_fusion
  (71 shorter events, 1.4 us)
Async XLA Ops:
  0.6 48.4 %copy-start = (bf16[8,1,128,128]{3,2,1,0:T(8,128)(2,1)S(1)}, bf16[8,1,128,128]{3,2,1,0:T(8,128)(2,1)}, u32[]{:S(2)}) copy-start(bf16[8,1,128,128]{3,2,1,0:T(8,128)(2,1)} %param.30) | copy-start | bytes 786436
  0.6 11.8 %copy-start.12 = (s32[32]{0:T(128)S(1)}, s32[32]{0:T(128)}, u32[]{:S(2)}) copy-start(s32[32]{0:T(128)} %param.35) | copy-start | bytes 388
  0.7 12.0 %copy-start.14 = (s32[8]{0:T(128)S(1)}, s32[8]{0:T(128)}, u32[]{:S(2)}) copy-start(s32[8]{0:T(128)} %param.37) | copy-start | bytes 100
  0.7 12.0 %copy-start.15 = (s32[1,8]{1,0:T(1,128)S(1)}, s32[1,8]{1,0:T(1,128)}, u32[]{:S(2)}) copy-start(s32[1,8]{1,0:T(1,128)} %param.34) | copy-start | bytes 100
  0.7 12.1 %copy-start.6 = (bf16[8,1,127,128]{3,0,2,1:T(8,128)(2,1)S(1)}, bf16[8,1,127,128]{3,0,2,1:T(8,128)(2,1)}, u32[]{:S(2)}) copy-start(bf16[8,1,127,128]{3,0,2,1:T(8,128)(2,1)} %param.32) | copy-start | bytes 780292
  0.7 12.1 %copy-start.7 = (bf16[8,1,127,128]{3,0,2,1:T(8,128)(2,1)S(1)}, bf16[8,1,127,128]{3,0,2,1:T(8,128)(2,1)}, u32[]{:S(2)}) copy-start(bf16[8,1,127,128]{3,0,2,1:T(8,128)(2,1)} %param.33) | copy-start | bytes 780292
  2.7 10.5 %copy-start.16 = (s32[5]{0:T(128)S(1)}, s32[5]{0:T(128)}, u32[]{:S(2)}) copy-start(s32[5]{0:T(128)} %param.36) | copy-start | bytes 64
  4.8 20.9 %all-to-all-start = ((f32[32,8,641]{2,1,0:T(8,128)}), f32[32,8,641]{2,1,0:T(8,128)S(1)}, u32[]{:S(2)}, u32[]{:S(2)}) async-start(f32[32,8,641]{2,1,0:T(8,128)} %pad_maximum_fusion.1), calls=%async_computation | async-start | bytes 1572864 | tf_op jit(solution)/shard_map/all_to_all | solution.py:37
  54.7 9.7 %copy-start.1 = (bf16[8,1,128,128]{3,2,0,1:T(8,128)(2,1)S(1)}, bf16[8,1,128,128]{3,2,0,1:T(8,128)(2,1)}, u32[]{:S(2)}) copy-start(bf16[8,1,128,128]{3,2,0,1:T(8,128)(2,1)} %get-tuple-element.66) | copy-start | bytes 786436
  55.4 9.6 %copy-start.4 = (bf16[8,1,128,128]{3,2,0,1:T(8,128)(2,1)S(1)}, bf16[8,1,128,128]{3,2,0,1:T(8,128)(2,1)}, u32[]{:S(2)}) copy-start(bf16[8,1,128,128]{3,2,0,1:T(8,128)(2,1)} %get-tuple-element.67) | copy-start | bytes 786436
  58.5 44.1 %copy-start.11 = (bf16[384,96]{0,1:T(8,128)(2,1)S(1)}, bf16[384,96]{0,1:T(8,128)(2,1)}, u32[]{:S(2)}) copy-start(bf16[384,96]{0,1:T(8,128)(2,1)} %param.25) | copy-start | bytes 221188
  58.5 67.7 %copy-start.3 = (bf16[1,256,96]{1,2,0:T(8,128)(2,1)S(1)}, bf16[1,256,96]{1,2,0:T(8,128)(2,1)}, u32[]{:S(2)}) copy-start(bf16[1,256,96]{1,2,0:T(8,128)(2,1)} %param.22) | copy-start | bytes 147460
  58.5 68.0 %copy-start.8 = (bf16[96,1024]{1,0:T(8,128)(2,1)S(1)}, bf16[96,1024]{1,0:T(8,128)(2,1)}, u32[]{:S(2)}) copy-start(bf16[96,1024]{1,0:T(8,128)(2,1)} %param.28) | copy-start | bytes 589828
  58.5 68.0 %copy-start.9 = (bf16[96,1024]{1,0:T(8,128)(2,1)S(1)}, bf16[96,1024]{1,0:T(8,128)(2,1)}, u32[]{:S(2)}) copy-start(bf16[96,1024]{1,0:T(8,128)(2,1)} %param.27) | copy-start | bytes 589828
  58.5 68.0 %copy-start.13 = (f32[96]{0:T(128)S(1)}, f32[96]{0:T(128)}, u32[]{:S(2)}) copy-start(f32[96]{0:T(128)} %param.26) | copy-start | bytes 1156
  58.5 19.0 %all-to-all-start.1 = ((f32[32,8,1,3,130]{4,1,3,2,0:T(8,128)}), f32[32,8,1,3,130]{4,1,3,2,0:T(8,128)S(1)}, u32[]{:S(2)}, u32[]{:S(2)}) async-start(f32[32,8,1,3,130]{4,1,3,2,0:T(8,128)} %maximum_bitcast_fusion), calls=%async_computation.1 | async-start | bytes 1572864 | tf_op jit(solution)/shard_map/all_to_all | solution.py:155
  64.5 62.5 %copy-start.2 = (bf16[8,1,128,128]{3,2,0,1:T(8,128)(2,1)}, bf16[8,1,128,128]{3,2,0,1:T(8,128)(2,1)S(1)}, u32[]{:S(2)}) copy-start(bf16[8,1,128,128]{3,2,0,1:T(8,128)(2,1)S(1)} %scatter.6) | copy-start | bytes 786436
  65.0 62.0 %copy-start.5 = (bf16[8,1,128,128]{3,2,0,1:T(8,128)(2,1)}, bf16[8,1,128,128]{3,2,0,1:T(8,128)(2,1)S(1)}, u32[]{:S(2)}) copy-start(bf16[8,1,128,128]{3,2,0,1:T(8,128)(2,1)S(1)} %scatter.9) | copy-start | bytes 786436
  102.8 5.3 %collective-permute-start = (f32[256,96]{0,1:T(8,128)S(1)}, f32[256,96]{0,1:T(8,128)S(1)}, u32[]{:S(2)}, u32[]{:S(2)}) collective-permute-start(f32[256,96]{0,1:T(8,128)S(1)} %fusion.62), channel_id=1, source_target_pairs={{0,32},{32,0},{64,96},{96,64},{128,160},{160,128},{192,224},{224,1... | collective-permute-start | bytes 294920 | tf_op jit(solution)/shard_map/ppermute | solution.py:22
  108.1 8.2 %collective-permute-start.1 = (f32[256,96]{0,1:T(8,128)S(1)}, f32[256,96]{0,1:T(8,128)S(1)}, u32[]{:S(2)}, u32[]{:S(2)}) collective-permute-start(f32[256,96]{0,1:T(8,128)S(1)} %add.109), channel_id=1, source_target_pairs={{0,64},{32,96},{64,0},{96,32},{128,192},{160,224},{192,128},{224,1... | collective-permute-start | bytes 294920 | tf_op jit(solution)/shard_map/ppermute | solution.py:22
  116.3 9.9 %collective-permute-start.2 = (f32[256,96]{0,1:T(8,128)S(1)}, f32[256,96]{0,1:T(8,128)S(1)}, u32[]{:S(2)}, u32[]{:S(2)}) collective-permute-start(f32[256,96]{0,1:T(8,128)S(1)} %add.110), channel_id=1, source_target_pairs={{0,128},{32,160},{64,192},{96,224},{128,0},{160,32},{192,64},{224,... | collective-permute-start | bytes 294920 | tf_op jit(solution)/shard_map/ppermute | solution.py:22
  127.2 58.3 %copy-start.10 = (bf16[1024,96]{0,1:T(8,128)(2,1)S(1)}, bf16[1024,96]{0,1:T(8,128)(2,1)}, u32[]{:S(2)}) copy-start(bf16[1024,96]{0,1:T(8,128)(2,1)} %param.29) | copy-start | bytes 589828
  185.8 5.1 %collective-permute-start.3 = (f32[256,96]{0,1:T(8,128)S(1)}, f32[256,96]{0,1:T(8,128)S(1)}, u32[]{:S(2)}, u32[]{:S(2)}) collective-permute-start(f32[256,96]{0,1:T(8,128)S(1)} %fusion.63), channel_id=1, source_target_pairs={{0,32},{32,0},{64,96},{96,64},{128,160},{160,128},{192,224},{224,1... | collective-permute-start | bytes 294920 | tf_op jit(solution)/shard_map/ppermute | solution.py:22
  190.9 8.1 %collective-permute-start.4 = (f32[256,96]{0,1:T(8,128)S(1)}, f32[256,96]{0,1:T(8,128)S(1)}, u32[]{:S(2)}, u32[]{:S(2)}) collective-permute-start(f32[256,96]{0,1:T(8,128)S(1)} %add.115), channel_id=1, source_target_pairs={{0,64},{32,96},{64,0},{96,32},{128,192},{160,224},{192,128},{224,1... | collective-permute-start | bytes 294920 | tf_op jit(solution)/shard_map/ppermute | solution.py:22
  199.0 10.6 %collective-permute-start.5 = (f32[256,96]{0,1:T(8,128)S(1)}, f32[256,96]{0,1:T(8,128)S(1)}, u32[]{:S(2)}, u32[]{:S(2)}) collective-permute-start(f32[256,96]{0,1:T(8,128)S(1)} %add.116), channel_id=1, source_target_pairs={{0,128},{32,160},{64,192},{96,224},{128,0},{160,32},{192,64},{224,... | collective-permute-start | bytes 294920 | tf_op jit(solution)/shard_map/ppermute | solution.py:22
where the time goes:
time: 211 us; the launch traced here: 210 us
  blocking collectives  104 us (49%)
  waiting for transfers between devices  49.7 us (24%)
  starting transfers between devices  32.7 us (15%)
  other arithmetic  10.9 us (5%)
  matrix products  6.5 us (3%)
  local copies, waits for them, and re-layouts  5.57 us (3%)
    all_to_all x1, blocking collectives, scatter_sum(): return jnp.sum(lax.all_to_all(pieces, axis, 0, 0, tiled=False), axis=0)  34.6 us
    ppermute x6, waiting for transfers between devices, exchange(): return lax.ppermute(value, axis, [(i, i ^ 1 << bit) for i in range(count)])  27.9 us
    all_gather x1, blocking collectives, body(): lax.all_gather(hidden, 'blk', axis=0, tiled=True)  23.3 us
    all_gather x1, blocking collectives, body(): lax.all_gather(heads_out, 'blk', axis=0, tiled=True)  23.1 us
    all_gather x1, blocking collectives, body(): query_rows = lax.all_gather(own_queries, 'blk', axis=0, tiled=True)  22.9 us
    ppermute x6, starting transfers between devices, exchange(): return lax.ppermute(value, axis, [(i, i ^ 1 << bit) for i in range(count)])  19.3 us
    all_to_all x1, waiting for transfers between devices, body(): parts = lax.all_to_all(packed, 'blk', 0, 0, tiled=False)  12.5 us
    all_to_all x1, waiting for transfers between devices, scatter_sum(): return jnp.sum(lax.all_to_all(pieces, axis, 0, 0, tiled=False), axis=0)  9.32 us
  transfers between devices with their start and end apart: 8, of which 8 were waited for; matrix products, arithmetic and copies ran while one was open for 2% of the time, Pallas kernels for 0%

commit v1 on v0

--- a/solution.py
+++ b/solution.py
@@ -123,7 +123,16 @@
     own_queries = rotate(own_proj[:, :, :group_queries], own_angle[:, None, None, :]).astype(
         jnp.bfloat16
     )
-    query_rows = lax.all_gather(own_queries, "blk", axis=0, tiled=True)
+    proceed_axis_part = lambda sheet: jnp.concatenate(
+        lax.all_to_all(
+            jnp.stack([sheet for _ in range(lax.axis_size("blk"))], axis=0),
+            axis_name="blk",
+            split_axis=0,
+            concat_axis=0,
+        ),
+        axis=0,
+    )
+    query_rows = proceed_axis_part(own_queries)
     new_key = rotate(own_proj[:, :, group_queries], own_angle[:, None, :]).astype(jnp.bfloat16)
     new_value = own_proj[:, :, group_queries + 1].astype(jnp.bfloat16)
     parent_rows = base_rows + parents[0]

time: 211 us -> 201 us (0.953)
  blocking collectives: 104 us -> 81 us
  waiting for transfers between devices: 49.7 us -> 56.9 us
  starting transfers between devices: 32.7 us -> 37.2 us
    all_gather x1 -> x0, blocking collectives: 22.9 us -> none  [body(): query_rows = lax.all_gather(own_queries, 'blk', axis=0, tiled=True)]
    all_to_all x0 -> x1, waiting for transfers between devices: none -> 7.09 us  [body(): lax.all_to_all(jnp.stack([sheet for _ in range(lax.axis_size('blk'))], ax...]
    all_to_all x0 -> x1, starting transfers between devices: none -> 5.01 us  [body(): lax.all_to_all(jnp.stack([sheet for _ in range(lax.axis_size('blk'))], ax...]
  transfers between devices with their start and end apart: 8 -> 9, of which waited for: 8 -> 9; matrix products, arithmetic and copies ran while one was open for 2% -> 2% of each run, Pallas kernels for 0% -> 0%
where the time goes in v1:
time: 201 us
  blocking collectives  81 us (40%)
  waiting for transfers between devices  56.9 us (28%)
  starting transfers between devices  37.2 us (19%)
  other arithmetic  10.9 us (5%)
  local copies, waits for them, and re-layouts  7 us (3%)
  matrix products  6.61 us (3%)
    all_to_all x1, blocking collectives, scatter_sum(): return jnp.sum(lax.all_to_all(pieces, axis, 0, 0, tiled=False), axis=0)  34.6 us
    ppermute x6, waiting for transfers between devices, exchange(): return lax.ppermute(value, axis, [(i, i ^ 1 << bit) for i in range(count)])  27.9 us
    all_gather x1, blocking collectives, body(): lax.all_gather(hidden, 'blk', axis=0, tiled=True)  23.3 us
    all_gather x1, blocking collectives, body(): lax.all_gather(heads_out, 'blk', axis=0, tiled=True)  23.1 us
    ppermute x6, starting transfers between devices, exchange(): return lax.ppermute(value, axis, [(i, i ^ 1 << bit) for i in range(count)])  19.3 us
    all_to_all x1, waiting for transfers between devices, body(): parts = lax.all_to_all(packed, 'blk', 0, 0, tiled=False)  12.6 us
    all_to_all x1, waiting for transfers between devices, scatter_sum(): return jnp.sum(lax.all_to_all(pieces, axis, 0, 0, tiled=False), axis=0)  9.32 us
    all_to_all x1, starting transfers between devices, scatter_sum(): return jnp.sum(lax.all_to_all(pieces, axis, 0, 0, tiled=False), axis=0)  7.62 us
  transfers between devices with their start and end apart: 9, of which 9 were waited for; matrix products, arithmetic and copies ran while one was open for 2% of the time, Pallas kernels for 0%

profile of v1, /device:TPU:2, one launch (start us, length us, event | category | flops | bytes accessed | tf_op | source)
XLA Modules:
  0.0 200.7 jit_solution(7584566865924731231)
XLA Ops:
  0.7 1.0 copy.175
  1.7 0.8 fusion.24
  2.5 0.2 concatenate.85
  2.7 1.1 fusion.22
  3.9 0.9 pad_maximum_fusion.1
  4.8 7.6 %all-to-all-start = ((f32[32,8,641]{2,1,0:T(8,128)}), f32[32,8,641]{2,1,0:T(8,128)S(1)}, u32[]{:S(2)}, u32[]{:S(2)}) async-start(f32[32,8,641]{2,1,0:T(8,128)} %pad_maximum_fusion.1), calls=%async_computation | async-start | bytes 1572864 | tf_op jit(solution)/shard_map/all_to_all | solution.py:37
  12.6 0.1 lt.33
  13.0 0.1 multiply_cosine_fusion.1
  13.3 0.6 gather_fusion
  13.9 0.6 gather_fusion.1
  14.5 0.1 convert_reduce_fusion
  14.6 1.0 compare_and_fusion
  15.6 0.9 bitcast_select_fusion.1
  16.5 9.3 %all-to-all-done = f32[32,8,641]{2,1,0:T(8,128)S(1)} async-done(((f32[32,8,641]{2,1,0:T(8,128)}), f32[32,8,641]{2,1,0:T(8,128)S(1)}, u32[]{:S(2)}, u32[]{:S(2)}) %all-to-all-start) | async-done | bytes 656416 | tf_op jit(solution)/shard_map/all_to_all | solution.py:37
  25.8 0.1 fusion.59
  26.2 0.7 stack.4
  26.9 5.0 %all-to-all-start.1 = ((bf16[32,8,1,3,128]{4,1,3,2,0:T(8,128)(2,1)}), bf16[32,8,1,3,128]{4,1,3,2,0:T(8,128)(2,1)S(1)}, u32[]{:S(2)}, u32[]{:S(2)}) async-start(bf16[32,8,1,3,128]{4,1,3,2,0:T(8,128)(2,1)} %stack.4), calls=%async_computation.1 | async-start | bytes 393216 | tf_op jit(solution)/shard_map/all_to_all | solution.py:127
  32.0 7.1 %all-to-all-done.1 = bf16[32,8,1,3,128]{4,1,3,2,0:T(8,128)(2,1)S(1)} async-done(((bf16[32,8,1,3,128]{4,1,3,2,0:T(8,128)(2,1)}), bf16[32,8,1,3,128]{4,1,3,2,0:T(8,128)(2,1)S(1)}, u32[]{:S(2)}, u32[]{:S(2)}) %all-to-all-start.1) | async-done | bytes 196640 | tf_op jit(solution)/shard_map/all_to_all | solution.py:127
  39.0 0.7 copy-done.3
  39.7 1.9 select_reduce_fusion
  41.6 0.1 concatenate.73
  41.7 3.1 %fusion.2 = (bf16[32,8,3,1024]{3,1,0,2:T(8,128)(2,1)}, f32[256,3]{0,1:T(4,128)S(1)}) fusion(f32[256,3,1024]{2,0,1:T(8,128)S(1)} %get-tuple-element.73, f32[256,3]{0,1:T(4,128)S(1)} %get-tuple-element.72, pred[256,1024]{1,0:T(8,128)(4,1)} %compare_and_fusion), kind=kLoop, calls=%fused_computation.8 | loop fusion | flops 3931392 | bytes 4986880 | tf_op jit(solution)/shard_map/reshape.476
  44.8 0.1 concatenate.74
  44.9 0.6 copy.183
  45.5 0.6 copy.182
  46.2 2.0 %fusion.5 = f32[32,8,1,3,128]{4,1,3,0,2:T(8,128)S(1)} fusion(bf16[1024,128,1,1]{1,0,3,2:T(8,128)(2,1)} %bitcast.110, bf16[32,8,3,1024]{3,1,0,2:T(8,128)(2,1)} %get-tuple-element.55), kind=kOutput, calls=%fused_computation.11 | convolution fusion | flops 201326592 | bytes 2228224 | tf_op jit(solution)/shard_map/kqn,knd->kqd/dot_general | solution.py:156
  48.2 1.1 maximum_bitcast_fusion
  49.3 5.2 %all-to-all-start.2 = ((f32[32,8,1,3,130]{4,1,3,2,0:T(8,128)}), f32[32,8,1,3,130]{4,1,3,2,0:T(8,128)S(1)}, u32[]{:S(2)}, u32[]{:S(2)}) async-start(f32[32,8,1,3,130]{4,1,3,2,0:T(8,128)} %maximum_bitcast_fusion), calls=%async_computation.2 | async-start | bytes 1572864 | tf_op jit(solution)/shard_map/all_to_all | solution.py:164
  54.5 0.1 fusion.61
  54.8 0.3 select_reduce_fusion.1
  55.1 0.1 copy.191
  55.3 12.6 %all-to-all-done.2 = f32[32,8,1,3,130]{4,1,3,2,0:T(8,128)S(1)} async-done(((f32[32,8,1,3,130]{4,1,3,2,0:T(8,128)}), f32[32,8,1,3,130]{4,1,3,2,0:T(8,128)S(1)}, u32[]{:S(2)}, u32[]{:S(2)}) %all-to-all-start.2) | async-done | bytes 399392 | tf_op jit(solution)/shard_map/all_to_all | solution.py:164
  67.9 0.2 fusion.67
  68.1 0.2 copy.206
  68.3 0.2 copy.207
  68.6 0.2 fusion.37
  68.9 0.2 fusion.38
  69.3 0.1 copy.186
  69.4 0.2 fusion.12
  69.6 0.2 fusion.10
  69.8 23.1 %all_gather.6 = bf16[256,384]{1,0:T(8,128)(2,1)S(1)} all-gather(bf16[8,384]{1,0:T(8,128)(2,1)S(1)} %bitcast.109), channel_id=1, replica_groups=mesh['kv'=8,'blk'=32] {'blk'}, dimensions={0}, use_global_device_ids=true | all-gather | bytes 202752 | tf_op jit(solution)/shard_map/all_gather | solution.py:198
  92.9 0.2 fusion.69
  93.1 2.0 collective-permute-start
  95.1 3.3 %collective-permute-done = f32[256,96]{0,1:T(8,128)S(1)} collective-permute-done((f32[256,96]{0,1:T(8,128)S(1)}, f32[256,96]{0,1:T(8,128)S(1)}, u32[]{:S(2)}, u32[]{:S(2)}) %collective-permute-start) | collective-permute-done | bytes 98336 | tf_op jit(solution)/shard_map/ppermute | solution.py:22
  98.5 3.4 %collective-permute-start.1 = (f32[256,96]{0,1:T(8,128)S(1)}, f32[256,96]{0,1:T(8,128)S(1)}, u32[]{:S(2)}, u32[]{:S(2)}) collective-permute-start(f32[256,96]{0,1:T(8,128)S(1)} %add.109), channel_id=1, source_target_pairs={{0,64},{32,96},{64,0},{96,32},{128,192},{160,224},{192,128},{224,1... | collective-permute-start | bytes 294920 | tf_op jit(solution)/shard_map/ppermute | solution.py:22
  101.8 4.8 %collective-permute-done.1 = f32[256,96]{0,1:T(8,128)S(1)} collective-permute-done((f32[256,96]{0,1:T(8,128)S(1)}, f32[256,96]{0,1:T(8,128)S(1)}, u32[]{:S(2)}, u32[]{:S(2)}) %collective-permute-start.1) | collective-permute-done | bytes 98336 | tf_op jit(solution)/shard_map/ppermute | solution.py:22
  106.6 6.3 %collective-permute-start.2 = (f32[256,96]{0,1:T(8,128)S(1)}, f32[256,96]{0,1:T(8,128)S(1)}, u32[]{:S(2)}, u32[]{:S(2)}) collective-permute-start(f32[256,96]{0,1:T(8,128)S(1)} %add.110), channel_id=1, source_target_pairs={{0,128},{32,160},{64,192},{96,224},{128,0},{160,32},{192,64},{224,... | collective-permute-start | bytes 294920 | tf_op jit(solution)/shard_map/ppermute | solution.py:22
  112.9 3.6 %collective-permute-done.2 = f32[256,96]{0,1:T(8,128)S(1)} collective-permute-done((f32[256,96]{0,1:T(8,128)S(1)}, f32[256,96]{0,1:T(8,128)S(1)}, u32[]{:S(2)}, u32[]{:S(2)}) %collective-permute-start.2) | collective-permute-done | bytes 98336 | tf_op jit(solution)/shard_map/ppermute | solution.py:22
  116.6 0.2 concatenate.86
  116.8 0.5 convolution_bitcast_fusion
  117.4 0.2 pad_maximum_fusion
  117.6 34.6 %all_to_all.20 = f32[32,8,2049]{2,1,0:T(8,128)S(1)} all-to-all(f32[32,8,2049]{2,1,0:T(8,128)S(1)} %pad_maximum_fusion), channel_id=1, replica_groups=mesh['kv'=8,'blk'=32] {'blk'}, dimensions={0} | all-to-all | bytes 4196352 | tf_op jit(solution)/shard_map/all_to_all | solution.py:37
  152.2 0.1 reduce_sum.89
  152.3 0.1 fusion.56
  152.4 0.1 fusion.29
  152.5 23.3 %all_gather.7 = bf16[256,1024]{1,0:T(8,128)(2,1)S(1)} all-gather(bf16[8,1024]{1,0:T(8,128)(2,1)S(1)} %fusion.29), channel_id=1, replica_groups=mesh['kv'=8,'blk'=32] {'blk'}, dimensions={0}, use_global_device_ids=true | all-gather | bytes 540672 | tf_op jit(solution)/shard_map/all_gather | solution.py:217
  175.8 0.3 fusion.70
  176.1 0.1 collective-permute-start.3
  176.2 5.0 %collective-permute-done.3 = f32[256,96]{0,1:T(8,128)S(1)} collective-permute-done((f32[256,96]{0,1:T(8,128)S(1)}, f32[256,96]{0,1:T(8,128)S(1)}, u32[]{:S(2)}, u32[]{:S(2)}) %collective-permute-start.3) | collective-permute-done | bytes 98336 | tf_op jit(solution)/shard_map/ppermute | solution.py:22
  181.3 3.3 %collective-permute-start.4 = (f32[256,96]{0,1:T(8,128)S(1)}, f32[256,96]{0,1:T(8,128)S(1)}, u32[]{:S(2)}, u32[]{:S(2)}) collective-permute-start(f32[256,96]{0,1:T(8,128)S(1)} %add.115), channel_id=1, source_target_pairs={{0,64},{32,96},{64,0},{96,32},{128,192},{160,224},{192,128},{224,1... | collective-permute-start | bytes 294920 | tf_op jit(solution)/shard_map/ppermute | solution.py:22
  184.6 4.8 %collective-permute-done.4 = f32[256,96]{0,1:T(8,128)S(1)} collective-permute-done((f32[256,96]{0,1:T(8,128)S(1)}, f32[256,96]{0,1:T(8,128)S(1)}, u32[]{:S(2)}, u32[]{:S(2)}) %collective-permute-start.4) | collective-permute-done | bytes 98336 | tf_op jit(solution)/shard_map/ppermute | solution.py:22
  189.4 4.3 %collective-permute-start.5 = (f32[256,96]{0,1:T(8,128)S(1)}, f32[256,96]{0,1:T(8,128)S(1)}, u32[]{:S(2)}, u32[]{:S(2)}) collective-permute-start(f32[256,96]{0,1:T(8,128)S(1)} %add.116), channel_id=1, source_target_pairs={{0,128},{32,160},{64,192},{96,224},{128,0},{160,32},{192,64},{224,... | collective-permute-start | bytes 294920 | tf_op jit(solution)/shard_map/ppermute | solution.py:22
  193.8 6.2 %collective-permute-done.5 = f32[256,96]{0,1:T(8,128)S(1)} collective-permute-done((f32[256,96]{0,1:T(8,128)S(1)}, f32[256,96]{0,1:T(8,128)S(1)}, u32[]{:S(2)}, u32[]{:S(2)}) %collective-permute-start.5) | collective-permute-done | bytes 98336 | tf_op jit(solution)/shard_map/ppermute | solution.py:22
  200.0 0.7 add_bitcast_fusion
  (76 shorter events, 1.6 us)
Async XLA Ops:
  0.6 39.1 %copy-start = (bf16[8,1,128,128]{3,2,1,0:T(8,128)(2,1)S(1)}, bf16[8,1,128,128]{3,2,1,0:T(8,128)(2,1)}, u32[]{:S(2)}) copy-start(bf16[8,1,128,128]{3,2,1,0:T(8,128)(2,1)} %param.30) | copy-start | bytes 786436
  0.6 11.9 %copy-start.13 = (s32[32]{0:T(128)S(1)}, s32[32]{0:T(128)}, u32[]{:S(2)}) copy-start(s32[32]{0:T(128)} %param.35) | copy-start | bytes 388
  0.7 12.0 %copy-start.15 = (s32[8]{0:T(128)S(1)}, s32[8]{0:T(128)}, u32[]{:S(2)}) copy-start(s32[8]{0:T(128)} %param.37) | copy-start | bytes 100
  0.7 12.0 %copy-start.16 = (s32[1,8]{1,0:T(1,128)S(1)}, s32[1,8]{1,0:T(1,128)}, u32[]{:S(2)}) copy-start(s32[1,8]{1,0:T(1,128)} %param.34) | copy-start | bytes 100
  0.7 12.1 %copy-start.7 = (bf16[8,1,127,128]{3,0,2,1:T(8,128)(2,1)S(1)}, bf16[8,1,127,128]{3,0,2,1:T(8,128)(2,1)}, u32[]{:S(2)}) copy-start(bf16[8,1,127,128]{3,0,2,1:T(8,128)(2,1)} %param.32) | copy-start | bytes 780292
  0.7 12.2 %copy-start.8 = (bf16[8,1,127,128]{3,0,2,1:T(8,128)(2,1)S(1)}, bf16[8,1,127,128]{3,0,2,1:T(8,128)(2,1)}, u32[]{:S(2)}) copy-start(bf16[8,1,127,128]{3,0,2,1:T(8,128)(2,1)} %param.33) | copy-start | bytes 780292
  2.7 10.5 %copy-start.17 = (s32[5]{0:T(128)S(1)}, s32[5]{0:T(128)}, u32[]{:S(2)}) copy-start(s32[5]{0:T(128)} %param.36) | copy-start | bytes 64
  4.8 20.9 %all-to-all-start = ((f32[32,8,641]{2,1,0:T(8,128)}), f32[32,8,641]{2,1,0:T(8,128)S(1)}, u32[]{:S(2)}, u32[]{:S(2)}) async-start(f32[32,8,641]{2,1,0:T(8,128)} %pad_maximum_fusion.1), calls=%async_computation | async-start | bytes 1572864 | tf_op jit(solution)/shard_map/all_to_all | solution.py:37
  26.9 12.1 %all-to-all-start.1 = ((bf16[32,8,1,3,128]{4,1,3,2,0:T(8,128)(2,1)}), bf16[32,8,1,3,128]{4,1,3,2,0:T(8,128)(2,1)S(1)}, u32[]{:S(2)}, u32[]{:S(2)}) async-start(bf16[32,8,1,3,128]{4,1,3,2,0:T(8,128)(2,1)} %stack.4), calls=%async_computation.1 | async-start | bytes 393216 | tf_op jit(solution)/shard_map/all_to_all | solution.py:127
  39.0 0.7 copy-start.3
  45.5 9.2 %copy-start.1 = (bf16[8,1,128,128]{3,2,0,1:T(8,128)(2,1)S(1)}, bf16[8,1,128,128]{3,2,0,1:T(8,128)(2,1)}, u32[]{:S(2)}) copy-start(bf16[8,1,128,128]{3,2,0,1:T(8,128)(2,1)} %get-tuple-element.68) | copy-start | bytes 786436
  46.2 9.1 %copy-start.5 = (bf16[8,1,128,128]{3,2,0,1:T(8,128)(2,1)S(1)}, bf16[8,1,128,128]{3,2,0,1:T(8,128)(2,1)}, u32[]{:S(2)}) copy-start(bf16[8,1,128,128]{3,2,0,1:T(8,128)(2,1)} %get-tuple-element.69) | copy-start | bytes 786436
  49.3 43.6 %copy-start.12 = (bf16[384,96]{0,1:T(8,128)(2,1)S(1)}, bf16[384,96]{0,1:T(8,128)(2,1)}, u32[]{:S(2)}) copy-start(bf16[384,96]{0,1:T(8,128)(2,1)} %param.25) | copy-start | bytes 221188
  49.3 67.3 %copy-start.4 = (bf16[1,256,96]{1,2,0:T(8,128)(2,1)S(1)}, bf16[1,256,96]{1,2,0:T(8,128)(2,1)}, u32[]{:S(2)}) copy-start(bf16[1,256,96]{1,2,0:T(8,128)(2,1)} %param.22) | copy-start | bytes 147460
  49.3 67.5 %copy-start.9 = (bf16[96,1024]{1,0:T(8,128)(2,1)S(1)}, bf16[96,1024]{1,0:T(8,128)(2,1)}, u32[]{:S(2)}) copy-start(bf16[96,1024]{1,0:T(8,128)(2,1)} %param.28) | copy-start | bytes 589828
  49.3 67.5 %copy-start.10 = (bf16[96,1024]{1,0:T(8,128)(2,1)S(1)}, bf16[96,1024]{1,0:T(8,128)(2,1)}, u32[]{:S(2)}) copy-start(bf16[96,1024]{1,0:T(8,128)(2,1)} %param.27) | copy-start | bytes 589828
  49.3 67.5 %copy-start.14 = (f32[96]{0:T(128)S(1)}, f32[96]{0:T(128)}, u32[]{:S(2)}) copy-start(f32[96]{0:T(128)} %param.26) | copy-start | bytes 1156
  49.3 18.6 %all-to-all-start.2 = ((f32[32,8,1,3,130]{4,1,3,2,0:T(8,128)}), f32[32,8,1,3,130]{4,1,3,2,0:T(8,128)S(1)}, u32[]{:S(2)}, u32[]{:S(2)}) async-start(f32[32,8,1,3,130]{4,1,3,2,0:T(8,128)} %maximum_bitcast_fusion), calls=%async_computation.2 | async-start | bytes 1572864 | tf_op jit(solution)/shard_map/all_to_all | solution.py:164
  54.8 62.5 %copy-start.2 = (bf16[8,1,128,128]{3,2,0,1:T(8,128)(2,1)}, bf16[8,1,128,128]{3,2,0,1:T(8,128)(2,1)S(1)}, u32[]{:S(2)}) copy-start(bf16[8,1,128,128]{3,2,0,1:T(8,128)(2,1)S(1)} %scatter.6) | copy-start | bytes 786436
  55.3 62.1 %copy-start.6 = (bf16[8,1,128,128]{3,2,0,1:T(8,128)(2,1)}, bf16[8,1,128,128]{3,2,0,1:T(8,128)(2,1)S(1)}, u32[]{:S(2)}) copy-start(bf16[8,1,128,128]{3,2,0,1:T(8,128)(2,1)S(1)} %scatter.9) | copy-start | bytes 786436
  93.1 5.3 %collective-permute-start = (f32[256,96]{0,1:T(8,128)S(1)}, f32[256,96]{0,1:T(8,128)S(1)}, u32[]{:S(2)}, u32[]{:S(2)}) collective-permute-start(f32[256,96]{0,1:T(8,128)S(1)} %fusion.69), channel_id=1, source_target_pairs={{0,32},{32,0},{64,96},{96,64},{128,160},{160,128},{192,224},{224,1... | collective-permute-start | bytes 294920 | tf_op jit(solution)/shard_map/ppermute | solution.py:22
  98.5 8.2 %collective-permute-start.1 = (f32[256,96]{0,1:T(8,128)S(1)}, f32[256,96]{0,1:T(8,128)S(1)}, u32[]{:S(2)}, u32[]{:S(2)}) collective-permute-start(f32[256,96]{0,1:T(8,128)S(1)} %add.109), channel_id=1, source_target_pairs={{0,64},{32,96},{64,0},{96,32},{128,192},{160,224},{192,128},{224,1... | collective-permute-start | bytes 294920 | tf_op jit(solution)/shard_map/ppermute | solution.py:22
  106.6 9.9 %collective-permute-start.2 = (f32[256,96]{0,1:T(8,128)S(1)}, f32[256,96]{0,1:T(8,128)S(1)}, u32[]{:S(2)}, u32[]{:S(2)}) collective-permute-start(f32[256,96]{0,1:T(8,128)S(1)} %add.110), channel_id=1, source_target_pairs={{0,128},{32,160},{64,192},{96,224},{128,0},{160,32},{192,64},{224,... | collective-permute-start | bytes 294920 | tf_op jit(solution)/shard_map/ppermute | solution.py:22
  117.6 58.3 %copy-start.11 = (bf16[1024,96]{0,1:T(8,128)(2,1)S(1)}, bf16[1024,96]{0,1:T(8,128)(2,1)}, u32[]{:S(2)}) copy-start(bf16[1024,96]{0,1:T(8,128)(2,1)} %param.29) | copy-start | bytes 589828
  176.1 5.1 %collective-permute-start.3 = (f32[256,96]{0,1:T(8,128)S(1)}, f32[256,96]{0,1:T(8,128)S(1)}, u32[]{:S(2)}, u32[]{:S(2)}) collective-permute-start(f32[256,96]{0,1:T(8,128)S(1)} %fusion.70), channel_id=1, source_target_pairs={{0,32},{32,0},{64,96},{96,64},{128,160},{160,128},{192,224},{224,1... | collective-permute-start | bytes 294920 | tf_op jit(solution)/shard_map/ppermute | solution.py:22
  181.3 8.1 %collective-permute-start.4 = (f32[256,96]{0,1:T(8,128)S(1)}, f32[256,96]{0,1:T(8,128)S(1)}, u32[]{:S(2)}, u32[]{:S(2)}) collective-permute-start(f32[256,96]{0,1:T(8,128)S(1)} %add.115), channel_id=1, source_target_pairs={{0,64},{32,96},{64,0},{96,32},{128,192},{160,224},{192,128},{224,1... | collective-permute-start | bytes 294920 | tf_op jit(solution)/shard_map/ppermute | solution.py:22
  189.4 10.6 %collective-permute-start.5 = (f32[256,96]{0,1:T(8,128)S(1)}, f32[256,96]{0,1:T(8,128)S(1)}, u32[]{:S(2)}, u32[]{:S(2)}) collective-permute-start(f32[256,96]{0,1:T(8,128)S(1)} %add.116), channel_id=1, source_target_pairs={{0,128},{32,160},{64,192},{96,224},{128,0},{160,32},{192,64},{224,... | collective-permute-start | bytes 294920 | tf_op jit(solution)/shard_map/ppermute | solution.py:22
